TPU v7x, 256 devices: a whole 4x4x8 slice. The times are simulated.
256 devices in a mesh: heads: 4 (over x), seq: 64 (over z, y, core).
Axes of the slice: x: 4, y: 4, z: 8, core: 2. Of those that a mesh axis runs over, the one named last changes fastest.
Arguments:
- queries: bfloat16 [32768, 2048], P('seq', 'heads'), may hold values from -64 to 64
- keys: bfloat16 [32768, 512], P('seq', 'heads'), may hold values from -6 to 6
- values: bfloat16 [32768, 512], P('seq', 'heads'), may hold values from -6 to 6
- vertical: int32 [16, 16], replicated, may hold values from 0 to 511, as said below
- slash: int32 [16, 8], replicated, may hold values from 0 to 15, as said below
- out_weight: bfloat16 [2048, 4096], P('heads'), may hold values from -0.25 to 0.25
Outputs:
- layer_out: bfloat16 [32768, 4096], P('seq', 'heads')
Inputs may be any that keep to these rules, and one draw needn't show every extreme that they name: `vertical`: each row lists 16 distinct blocks; the four rows of one KV head (rows 4g to 4g+3) list 64 distinct blocks in all; at most 2 of those lie within blocks k * 8 to (k + 1) * 8 - 1 for any k, and in every draw some k reaches 2. `slash`: each row lists 8 distinct offsets, 0 among them; some row holds 15 in every draw.
All inputs are finite; a program needn't handle non-finite values.
Results may differ from a plain program's by a relative error of at most 0.0095.
Values may be sent and summed in bfloat16 or wider, within the bound.
No kernel may reach another device: no remote copies, remote signals or barrier semaphores. Data moves between devices by JAX's collectives and lax.ppermute only.
A program may use at most 128 MiB of HBM per device.

v0:
```python
import math
import jax
import jax.numpy as jnp
import numpy as np
from jax import lax
from jax.sharding import Mesh
from jax.sharding import PartitionSpec as P

HEAD_SIZE = 128
BLOCK_TOKENS = 64
SEQ = ("z", "y", "core")


def shift(block, axis, size, distance):
    route = [(i, i + distance) for i in range(size) if 0 <= i + distance < size]
    return lax.ppermute(block, axis, route)


def ring(block, axis, size, distance):
    return lax.ppermute(block, axis, [(i, (i + distance) % size) for i in range(size)])


def spread(table, rows, cols):
    return jnp.repeat(jnp.repeat(table, rows, axis=-2), cols, axis=-1)


def make_local(sizes):
    heads_n, z_n, y_n, core_n = sizes
    cycle_size = z_n * y_n * core_n

    def local(queries, keys, values, vertical, slash, out_weight):
        head_dim = HEAD_SIZE
        local_heads = queries.shape[1] // head_dim
        token_count = queries.shape[0]
        block_count = token_count // BLOCK_TOKENS
        score_scale = 1.0 / math.sqrt(head_dim)
        kv_group = lax.axis_index("heads")
        core = lax.axis_index("core")
        cycle_index = lax.axis_index(SEQ)
        vert_group = lax.dynamic_slice_in_dim(vertical, kv_group * local_heads, local_heads, 0)
        slash_group = lax.dynamic_slice_in_dim(slash, kv_group * local_heads, local_heads, 0)
        union_list = vert_group.reshape(-1)
        listed_count = union_list.shape[0]
        owner_dev = union_list // block_count
        within_dev = union_list % block_count
        paired = jnp.stack([keys, values]).reshape(2, block_count, BLOCK_TOKENS, head_dim)
        owned_here = owner_dev == cycle_index
        capacity = min(block_count, max(2, 2 * listed_count // cycle_size))
        positions = jnp.arange(listed_count)
        same_owner = (owner_dev[:, None] == owner_dev[None, :]) & (
            positions[None, :] < positions[:, None]
        )
        slot_index = jnp.sum(same_owner.astype(jnp.int32), axis=1)
        selector = owned_here[None, :] & (slot_index[None, :] == jnp.arange(capacity)[:, None])
        picked = jnp.sum(jnp.where(selector, within_dev[None, :], 0), axis=1)
        outgoing = paired[:, picked].reshape(2, capacity * BLOCK_TOKENS, head_dim)
        arrived = lax.all_gather(outgoing, SEQ, axis=1, tiled=True)
        rows_total, width = out_weight.shape
        col_width = width // heads_n
        half_rows = rows_total // core_n
        fetched = []
        for distance in range(1, heads_n):
            dest_cols = (kv_group + distance) % heads_n * col_width
            piece = lax.dynamic_slice(
                out_weight, (core * half_rows, dest_cols), (half_rows, col_width)
            )
            fetched.append(ring(piece, "heads", heads_n, distance))
        fetched = jnp.stack(fetched)
        sibling_w = ring(fetched, "core", core_n, 1)
        own_w = lax.dynamic_slice(out_weight, (0, kv_group * col_width), (rows_total, col_width))
        earlier = shift(paired, SEQ, cycle_size, 1)
        farther = shift(paired, SEQ, cycle_size, 2)
        context = jnp.concatenate([farther, earlier, paired], axis=1)
        context_blocks = context.shape[1]
        context_k = context[0].reshape(context_blocks * BLOCK_TOKENS, head_dim)
        context_v = context[1].reshape(context_blocks * BLOCK_TOKENS, head_dim)
        first_block = cycle_index * block_count
        query_block = first_block + jnp.arange(block_count, dtype=jnp.int32)
        key_block = (
            first_block
            - (context_blocks - block_count)
            + jnp.arange(context_blocks, dtype=jnp.int32)
        )
        distance_blk = query_block[:, None] - key_block[None, :]
        token_pos = jnp.arange(BLOCK_TOKENS)
        causal_tri = token_pos[None, :] <= token_pos[:, None]
        causal_ctx = jnp.tile(causal_tri, (block_count, context_blocks))
        query_heads = queries.reshape(token_count, local_heads, head_dim).transpose(1, 0, 2)
        score_diag = (
            jnp.einsum("htd,ud->htu", query_heads, context_k, preferred_element_type=jnp.float32)
            * score_scale
        )
        in_slash = jnp.any(distance_blk[None, None] == slash_group[:, :, None, None], axis=1)
        in_vert = jnp.any(key_block[None, None, :] == vert_group[:, :, None], axis=1)
        keep_blk = in_slash & (key_block >= 0)[None, None, :] & jnp.logical_not(in_vert)[:, None, :]
        whole_blk = keep_blk & (distance_blk != 0)[None]
        allow_diag = (
            spread(whole_blk, BLOCK_TOKENS, BLOCK_TOKENS)
            | spread(keep_blk & (distance_blk == 0)[None], BLOCK_TOKENS, BLOCK_TOKENS)
            & causal_ctx[None]
        )
        top_diag = jnp.max(jnp.where(allow_diag, score_diag, -jnp.inf), axis=2, keepdims=True)
        expo_diag = jnp.where(allow_diag, jnp.exp(score_diag - top_diag), 0.0)
        total_diag = jnp.sum(expo_diag, axis=2, keepdims=True)
        acc_diag = jnp.einsum(
            "htu,ud->htd",
            expo_diag.astype(jnp.bfloat16),
            context_v,
            preferred_element_type=jnp.float32,
        )
        arrived = arrived.reshape(2, cycle_size * capacity, BLOCK_TOKENS, head_dim)
        chosen = arrived[:, owner_dev * capacity + slot_index]
        vert_count = vert_group.shape[1]
        chosen = chosen.reshape(2, local_heads, vert_count * BLOCK_TOKENS, head_dim)
        score_vert = (
            jnp.einsum("htd,hud->htu", query_heads, chosen[0], preferred_element_type=jnp.float32)
            * score_scale
        )
        vert_cols = jnp.repeat(vert_group, BLOCK_TOKENS, axis=1)
        row_block = jnp.repeat(query_block, BLOCK_TOKENS)
        causal_vert = jnp.tile(causal_tri, (block_count, vert_count))
        allow_vert = (vert_cols[:, None, :] < row_block[None, :, None]) | (
            vert_cols[:, None, :] == row_block[None, :, None]
        ) & causal_vert[None]
        top_vert = jnp.max(jnp.where(allow_vert, score_vert, -jnp.inf), axis=2, keepdims=True)
        row_top = jnp.maximum(top_diag, top_vert)
        expo_vert = jnp.where(allow_vert, jnp.exp(score_vert - row_top), 0.0)
        diag_scale = jnp.exp(top_diag - row_top)
        row_total = total_diag * diag_scale + jnp.sum(expo_vert, axis=2, keepdims=True)
        acc_vert = jnp.einsum(
            "htu,hud->htd",
            expo_vert.astype(jnp.bfloat16),
            chosen[1],
            preferred_element_type=jnp.float32,
        )
        head_out = (acc_diag * diag_scale + acc_vert) / row_total
        attention = head_out.astype(jnp.bfloat16).transpose(1, 0, 2).reshape(token_count, -1)
        total = jnp.dot(attention, own_w, preferred_element_type=jnp.float32)
        for distance in range(1, heads_n):
            other = ring(attention, "heads", heads_n, distance)
            mine = lax.dynamic_slice_in_dim(other, core * half_rows, half_rows, 1)
            theirs = lax.dynamic_slice_in_dim(other, (1 - core) * half_rows, half_rows, 1)
            total = total + jnp.dot(mine, fetched[distance - 1], preferred_element_type=jnp.float32)
            total = total + jnp.dot(
                theirs, sibling_w[distance - 1], preferred_element_type=jnp.float32
            )
        return total.astype(jnp.bfloat16)

    return local


def split_mesh(mesh):
    devices = mesh.devices
    heads_n, seq_n = devices.shape
    core_n = 2
    y_n = len({d.coords[1] for d in devices.flat})
    z_n = seq_n // (core_n * y_n)
    sizes = (heads_n, z_n, y_n, core_n)
    return (Mesh(np.asarray(devices).reshape(sizes), ("heads",) + SEQ), sizes)


def solution(mesh):
    sub, sizes = split_mesh(mesh)
    return jax.shard_map(
        make_local(sizes),
        mesh=sub,
        in_specs=(P(SEQ, "heads"), P(SEQ, "heads"), P(SEQ, "heads"), P(), P(), P("heads", None)),
        out_specs=P(SEQ, "heads"),
        check_vma=False,
    )
```

profile of v0, /device:TPU:1, one launch (start us, length us, event | category | flops | bytes accessed | tf_op | source)
XLA Modules:
  0.0 151.8 jit_solution(9992068218329997265)
XLA Ops:
  7.7 1.7 %pad_maximum_fusion.1 = bf16[2,8,64,128]{3,2,1,0:T(8,128)(2,1)} fusion(bf16[1,8,64,128]{3,2,1,0:T(8,128)(2,1)} %bitcast.175, bf16[1,8,64,128]{3,2,1,0:T(8,128)(2,1)} %bitcast.177), kind=kLoop, calls=%fused_computation.41 | loop fusion | flops 131072 | bytes 524288 | tf_op jit(solution)/shard_map/stack | solution.py:46
  9.4 1.5 gather_fusion
  11.6 4.6 %collective-permute-start.1 = (bf16[2,8,64,128]{3,2,1,0:T(8,128)(2,1)}, bf16[2,8,64,128]{3,2,1,0:T(8,128)(2,1)}, u32[]{:S(2)}, u32[]{:S(2)}) collective-permute-start(bf16[2,8,64,128]{3,2,1,0:T(8,128)(2,1)} %pad_maximum_fusion.1), channel_id=1, source_target_pairs={{0,1},{1,2},{2,3},{3,4},{4,5},{5,6},{6,7},{7,8},{8,9},{9,10},{10,1... | collective-permute-start | bytes 786440 | tf_op jit(solution)/shard_map/ppermute | solution.py:16
  16.2 3.9 %collective-permute-start = (bf16[2,8,64,128]{3,2,1,0:T(8,128)(2,1)}, bf16[2,8,64,128]{3,2,1,0:T(8,128)(2,1)}, u32[]{:S(2)}, u32[]{:S(2)}) collective-permute-start(bf16[2,8,64,128]{3,2,1,0:T(8,128)(2,1)} %pad_maximum_fusion.1), channel_id=1, source_target_pairs={{0,2},{1,3},{2,4},{3,5},{4,6},{5,7},{6,8},{7,9},{8,10},{9,11},{10,... | collective-permute-start | bytes 786440 | tf_op jit(solution)/shard_map/ppermute | solution.py:16
  20.1 2.5 %fusion.57 = (bf16[256,1024]{1,0:T(8,128)(2,1)}, bf16[256,1024]{1,0:T(8,128)(2,1)}, bf16[256,1024]{1,0:T(8,128)(2,1)}) fusion(bf16[512,4096]{1,0:T(8,128)(2,1)} %param.11, s32[]{:T(128)S(6)} %select_n.128, s32[]{:T(128)S(6)} %select_n.130, s32[]{:T(128)S(6)} %select_n.135, s32[]{:T(128)S(6)} %select_n.133), kind=kLoop, calls=%fused_computation.100 | loop fusion | bytes 3145744 | tf_op jit(solution)/shard_map/dynamic_slice | solution.py:64
  22.6 2.5 %collective-permute-start.5 = (bf16[256,1024]{1,0:T(8,128)(2,1)}, bf16[256,1024]{1,0:T(8,128)(2,1)}, u32[]{:S(2)}, u32[]{:S(2)}) collective-permute-start(bf16[256,1024]{1,0:T(8,128)(2,1)} %get-tuple-element.12), channel_id=1, source_target_pairs={{0,192},{64,0},{128,64},{192,128},{1,193},{65,1},{129,65},{193,129... | collective-permute-start | bytes 1572872 | tf_op jit(solution)/shard_map/ppermute | solution.py:20
  27.6 2.1 %and.141 = pred[512,1536]{0,1:T(8,128)(4,1)S(1)} reshape(pred[8,64,24,64]{1,0,3,2:T(8,128)(4,1)S(1)} %tile.4) | data formatting | bytes 1572864 | tf_op jit(solution)/shard_map/and | solution.py:99
  35.8 3.4 %fusion = (f32[4,512]{1,0:T(4,128)S(1)}, f32[1536,4,512]{2,0,1:T(8,128)S(1)}) fusion(pred[512,1536]{0,1:T(8,128)(4,1)S(1)} %and.141, pred[4,512,24]{1,2,0:T(8,128)(4,1)S(1)} %reshape.357, pred[4,512,24]{1,2,0:T(8,128)(4,1)S(1)} %reshape.355, bf16[1536,128,1]{1,0,2:T(8,128)(2,1)S(1)} %bitcast.167, bf16[512,512]{1,0:T(8,128)(2,1)S(1)} %copy-done), kind=kOutput, calls=%fused_computation.4 | convolution fusion | flops 821032960 | bytes 14393344 | tf_op jit(solution)/shard_map/htd,ud->htu/dot_general | solution.py:90
  39.2 5.7 %fusion.7 = (f32[4,512]{1,0:T(4,128)S(1)}, bf16[4,512,1536]{1,2,0:T(8,128)(2,1)}) fusion(f32[1536,4,512]{2,0,1:T(8,128)S(1)} %get-tuple-element.23, f32[4,512]{1,0:T(4,128)S(1)} %get-tuple-element.22, pred[512,1536]{0,1:T(8,128)(4,1)S(1)} %and.141, pred[4,512,24]{1,2,0:T(8,128)(4,1)S(1)} %reshape.357, pred[4,512,24]{1,2,0:T(8,128)(4,1)S(1)} %reshape.355), kind=kLoop, calls=%fused_computation.15 | loop fusion | flops 22018048 | bytes 19775488 | tf_op jit(solution)/shard_map/reduce_sum | solution.py:104
  44.8 3.2 %collective-permute-done.5 = bf16[256,1024]{1,0:T(8,128)(2,1)} collective-permute-done((bf16[256,1024]{1,0:T(8,128)(2,1)}, bf16[256,1024]{1,0:T(8,128)(2,1)}, u32[]{:S(2)}, u32[]{:S(2)}) %collective-permute-start.5) | collective-permute-done | bytes 524320 | tf_op jit(solution)/shard_map/ppermute | solution.py:20
  48.0 3.9 %collective-permute-done.3 = bf16[256,1024]{1,0:T(8,128)(2,1)} collective-permute-done((bf16[256,1024]{1,0:T(8,128)(2,1)}, bf16[256,1024]{1,0:T(8,128)(2,1)}, u32[]{:S(2)}, u32[]{:S(2)}) %collective-permute-start.3) | collective-permute-done | bytes 524320 | tf_op jit(solution)/shard_map/ppermute | solution.py:20
  51.9 2.7 %pad_maximum_fusion = bf16[3,256,1024]{2,1,0:T(8,128)(2,1)} fusion(bf16[1,256,1024]{2,1,0:T(8,128)(2,1)} %bitcast.30, bf16[1,256,1024]{2,1,0:T(8,128)(2,1)} %bitcast.29, bf16[1,256,1024]{2,1,0:T(8,128)(2,1)} %bitcast.28), kind=kLoop, calls=%fused_computation.21 | loop fusion | flops 1572864 | bytes 3145728 | tf_op jit(solution)/shard_map/stack | solution.py:68
  55.1 40.0 %all-gather.2.cloned.1.call-done = bf16[2,8192,128]{2,1,0:T(8,128)(2,1)} async-done(((bf16[2,128,128]{2,1,0:T(8,128)(2,1)}), bf16[2,8192,128]{2,1,0:T(8,128)(2,1)}) %all-gather.2.cloned.1.call-update) | async-done | bytes 4194320 | tf_op jit(solution)/shard_map/all_gather | solution.py:57
  95.1 3.3 %gather_fusion.1 = bf16[64,2,64,128]{3,2,1,0:T(8,128)(2,1)S(1)} fusion(bf16[2,128,64,128]{3,2,1,0:T(8,128)(2,1)} %bitcast.172, s32[1024]{0:T(1024)} %pad_clamp_fusion), kind=kCustom, calls=%fused_computation.1 | custom fusion | bytes 4194560 | tf_op jit(solution)/shard_map/gather | solution.py:112
  99.1 3.0 %fusion.4 = (f32[4,512]{1,0:T(4,128)S(1)}, f32[4,1024,512]{2,1,0:T(8,128)S(1)}) fusion(pred[512,1024]{0,1:T(8,128)(4,1)S(1)} %and.144, s32[512]{0:T(512)S(1)} %copy-done.5, s32[4,1024]{1,0:T(4,128)S(1)} %copy-done.4, bf16[4,1024,128]{2,1,0:T(8,128)(2,1)S(1)} %bitcast.174, bf16[512,512]{1,0:T(8,128)(2,1)S(1)} %copy-done), kind=kOutput, calls=%fused_computation.11 | convolution fusion | flops 551548928 | bytes 10512384 | tf_op jit(solution)/shard_map/htd,hud->htu/dot_general | solution.py:116
  102.1 3.8 %fusion.9 = f32[4,512]{1,0:T(4,128)S(1)} fusion(f32[4,1024,512]{2,1,0:T(8,128)S(1)} %get-tuple-element.25, f32[4,512]{1,0:T(4,128)S(1)} %max.19, pred[512,1024]{0,1:T(8,128)(4,1)S(1)} %and.144, s32[512]{0:T(512)S(1)} %copy-done.5, s32[4,1024]{1,0:T(4,128)S(1)} %copy-done.4), kind=kLoop, calls=%fused_computation.17 | loop fusion | flops 16775168 | bytes 8947712 | tf_op jit(solution)/shard_map/reduce_sum | solution.py:129
  107.1 3.8 %divide_convert_fusion = bf16[512,4,128]{0,2,1:T(8,128)(2,1)S(1)} fusion(f32[512,4,128]{0,2,1:T(8,128)S(1)} %fusion.16, bf16[4,1024,128]{2,1,0:T(8,128)(2,1)S(1)} %bitcast.173, f32[4,1024,512]{2,1,0:T(8,128)S(1)} %get-tuple-element.25, f32[4,512]{1,0:T(4,128)S(1)} %max.19, f32[512,4]{0,1:T(4,128)S(1)} %get-tuple-element.5, s32[512]{0:T(512)S(1)} %copy-done.5, ...), kind=kOutput, calls=%fused_computation.28 | convolution fusion | flops 554434560 | bytes 11569152 | tf_op jit(solution)/shard_map/htu,hud->htd/dot_general | solution.py:130
  110.9 2.8 %collective-permute-start.7 = (bf16[512,512]{0,1:T(8,128)(2,1)S(1)}, bf16[512,512]{0,1:T(8,128)(2,1)S(1)}, u32[]{:S(2)}, u32[]{:S(2)}) collective-permute-start(bf16[512,512]{0,1:T(8,128)(2,1)S(1)} %bitcast.168), channel_id=1, source_target_pairs={{0,128},{64,192},{128,0},{192,64},{1,129},{65,193},{129,1},{193,65... | collective-permute-start | bytes 1572872 | tf_op jit(solution)/shard_map/ppermute | solution.py:20
  115.2 1.9 %fusion.20 = f32[512,1024]{1,0:T(8,128)S(1)} fusion(bf16[512,512]{0,1:T(8,128)(2,1)S(1)} %bitcast.171, bf16[512,4096]{1,0:T(8,128)(2,1)} %param.11, s32[]{:T(128)S(6)} %select_n.127), kind=kOutput, calls=%fused_computation.26 | convolution fusion | flops 536870912 | bytes 3670020 | tf_op jit(solution)/shard_map/dot_general | solution.py:138
  117.1 8.6 %collective-permute-done.7 = bf16[512,512]{0,1:T(8,128)(2,1)S(1)} collective-permute-done((bf16[512,512]{0,1:T(8,128)(2,1)S(1)}, bf16[512,512]{0,1:T(8,128)(2,1)S(1)}, u32[]{:S(2)}, u32[]{:S(2)}) %collective-permute-start.7) | collective-permute-done | bytes 524320 | tf_op jit(solution)/shard_map/ppermute | solution.py:20
  127.2 1.5 fusion.27
  128.8 8.8 %collective-permute-done.2 = bf16[512,512]{0,1:T(8,128)(2,1)S(1)} collective-permute-done((bf16[512,512]{0,1:T(8,128)(2,1)S(1)}, bf16[512,512]{0,1:T(8,128)(2,1)S(1)}, u32[]{:S(2)}, u32[]{:S(2)}) %collective-permute-start.2) | collective-permute-done | bytes 524320 | tf_op jit(solution)/shard_map/ppermute | solution.py:20
  139.1 1.5 fusion.38
  142.1 2.8 %add_convert_fusion = bf16[512,1024]{1,0:T(8,128)(2,1)} fusion(f32[512,1024]{1,0:T(8,128)S(1)} %fusion.32, f32[512,1024]{1,0:T(8,128)S(1)} %fusion.27, f32[512,1024]{1,0:T(8,128)S(1)} %fusion.35, f32[512,1024]{1,0:T(8,128)S(1)} %fusion.28, f32[512,1024]{1,0:T(8,128)S(1)} %fusion.20, f32[512,1024]{1,0:T(8,128)S(1)} %fusion.38, ...), kind=kOutput, calls=%fused_computation.20 | convolution fusion | flops 272105472 | bytes 14417924 | tf_op jit(solution)/shard_map/dot_general | solution.py:144
  (77 shorter events, 18.4 us)
Async XLA Ops:
  6.5 29.2 %copy-start = (bf16[512,512]{1,0:T(8,128)(2,1)S(1)}, bf16[512,512]{1,0:T(8,128)(2,1)}, u32[]{:S(2)}) copy-start(bf16[512,512]{1,0:T(8,128)(2,1)} %param.6) | copy-start | bytes 1572868
  6.5 19.8 %copy-start.6 = (s32[16,8]{0,1:T(8,128)S(1)}, s32[16,8]{0,1:T(8,128)}, u32[]{:S(2)}) copy-start(s32[16,8]{0,1:T(8,128)} %param.10) | copy-start | bytes 1540
  6.5 88.5 %all-gather.2.cloned.1.call-start = ((), (), s32[]{:S(2)}) async-start(), calls=%async_computation | async-start | bytes 4259840 | tf_op jit(solution)/shard_map/all_gather | solution.py:57
  11.6 23.0 %collective-permute-start.1 = (bf16[2,8,64,128]{3,2,1,0:T(8,128)(2,1)}, bf16[2,8,64,128]{3,2,1,0:T(8,128)(2,1)}, u32[]{:S(2)}, u32[]{:S(2)}) collective-permute-start(bf16[2,8,64,128]{3,2,1,0:T(8,128)(2,1)} %pad_maximum_fusion.1), channel_id=1, source_target_pairs={{0,1},{1,2},{2,3},{3,4},{4,5},{5,6},{6,7},{7,8},{8,9},{9,10},{10,1... | collective-permute-start | bytes 786440 | tf_op jit(solution)/shard_map/ppermute | solution.py:16
  16.2 18.4 %collective-permute-start = (bf16[2,8,64,128]{3,2,1,0:T(8,128)(2,1)}, bf16[2,8,64,128]{3,2,1,0:T(8,128)(2,1)}, u32[]{:S(2)}, u32[]{:S(2)}) collective-permute-start(bf16[2,8,64,128]{3,2,1,0:T(8,128)(2,1)} %pad_maximum_fusion.1), channel_id=1, source_target_pairs={{0,2},{1,3},{2,4},{3,5},{4,6},{5,7},{6,8},{7,9},{8,10},{9,11},{10,... | collective-permute-start | bytes 786440 | tf_op jit(solution)/shard_map/ppermute | solution.py:16
  22.6 25.4 %collective-permute-start.5 = (bf16[256,1024]{1,0:T(8,128)(2,1)}, bf16[256,1024]{1,0:T(8,128)(2,1)}, u32[]{:S(2)}, u32[]{:S(2)}) collective-permute-start(bf16[256,1024]{1,0:T(8,128)(2,1)} %get-tuple-element.12), channel_id=1, source_target_pairs={{0,192},{64,0},{128,64},{192,128},{1,193},{65,1},{129,65},{193,129... | collective-permute-start | bytes 1572872 | tf_op jit(solution)/shard_map/ppermute | solution.py:20
  25.1 22.9 %collective-permute-start.4 = (bf16[256,1024]{1,0:T(8,128)(2,1)}, bf16[256,1024]{1,0:T(8,128)(2,1)}, u32[]{:S(2)}, u32[]{:S(2)}) collective-permute-start(bf16[256,1024]{1,0:T(8,128)(2,1)} %get-tuple-element.13), channel_id=1, source_target_pairs={{0,128},{64,192},{128,0},{192,64},{1,129},{65,193},{129,1},{193,65... | collective-permute-start | bytes 1572872 | tf_op jit(solution)/shard_map/ppermute | solution.py:20
  25.6 26.3 %collective-permute-start.3 = (bf16[256,1024]{1,0:T(8,128)(2,1)}, bf16[256,1024]{1,0:T(8,128)(2,1)}, u32[]{:S(2)}, u32[]{:S(2)}) collective-permute-start(bf16[256,1024]{1,0:T(8,128)(2,1)} %get-tuple-element.11), channel_id=1, source_target_pairs={{0,64},{64,128},{128,192},{192,0},{1,65},{65,129},{129,193},{193,1... | collective-permute-start | bytes 1572872 | tf_op jit(solution)/shard_map/ppermute | solution.py:20
  27.6 7.0 %copy-start.2 = (bf16[512,128]{1,0:T(8,128)(2,1)S(1)}, bf16[512,128]{1,0:T(8,128)(2,1)}, u32[]{:S(2)}) copy-start(bf16[512,128]{1,0:T(8,128)(2,1)} %param.8) | copy-start | bytes 393220
  29.7 4.9 %copy-start.3 = (bf16[512,128]{1,0:T(8,128)(2,1)S(1)}, bf16[512,128]{1,0:T(8,128)(2,1)}, u32[]{:S(2)}) copy-start(bf16[512,128]{1,0:T(8,128)(2,1)} %param.7) | copy-start | bytes 393220
  54.7 72.6 %collective-permute-start.6 = (bf16[3,256,1024]{2,1,0:T(8,128)(2,1)}, bf16[3,256,1024]{2,1,0:T(8,128)(2,1)}, u32[]{:S(2)}, u32[]{:S(2)}) collective-permute-start(bf16[3,256,1024]{2,1,0:T(8,128)(2,1)} %pad_maximum_fusion), channel_id=1, source_target_pairs={{0,1},{1,0},{2,3},{3,2},{4,5},{5,4},{6,7},{7,6},{8,9},{9,8},{10,11... | collective-permute-start | bytes 4718600 | tf_op jit(solution)/shard_map/ppermute | solution.py:20
  98.3 0.7 copy-start.4
  98.3 0.7 copy-start.5
  98.4 7.6 %slice-start = ((s8[6291456]{0:T(1024)(128)(4,1)}), s8[4194304]{0:T(1024)(128)(4,1)S(1)}, s32[]{:S(2)}) async-start(s8[6291456]{0:T(1024)(128)(4,1)} %bitcast.165), calls=%async_computation.1 | async-start | bytes 8388608
  99.1 6.9 %slice-start.1 = ((s8[6291456]{0:T(1024)(128)(4,1)}), s8[2097152]{0:T(1024)(128)(4,1)S(1)}, s32[]{:S(2)}) async-start(s8[6291456]{0:T(1024)(128)(4,1)} %bitcast.165), calls=%async_computation.2 | async-start | bytes 4194304
  110.9 14.8 %collective-permute-start.7 = (bf16[512,512]{0,1:T(8,128)(2,1)S(1)}, bf16[512,512]{0,1:T(8,128)(2,1)S(1)}, u32[]{:S(2)}, u32[]{:S(2)}) collective-permute-start(bf16[512,512]{0,1:T(8,128)(2,1)S(1)} %bitcast.168), channel_id=1, source_target_pairs={{0,128},{64,192},{128,0},{192,64},{1,129},{65,193},{129,1},{193,65... | collective-permute-start | bytes 1572872 | tf_op jit(solution)/shard_map/ppermute | solution.py:20
  113.7 26.9 %collective-permute-start.8 = (bf16[512,512]{0,1:T(8,128)(2,1)S(1)}, bf16[512,512]{0,1:T(8,128)(2,1)S(1)}, u32[]{:S(2)}, u32[]{:S(2)}) collective-permute-start(bf16[512,512]{0,1:T(8,128)(2,1)S(1)} %bitcast.169), channel_id=1, source_target_pairs={{0,192},{64,0},{128,64},{192,128},{1,193},{65,1},{129,65},{193,129... | collective-permute-start | bytes 1572872 | tf_op jit(solution)/shard_map/ppermute | solution.py:20
  114.6 23.0 %collective-permute-start.2 = (bf16[512,512]{0,1:T(8,128)(2,1)S(1)}, bf16[512,512]{0,1:T(8,128)(2,1)S(1)}, u32[]{:S(2)}, u32[]{:S(2)}) collective-permute-start(bf16[512,512]{0,1:T(8,128)(2,1)S(1)} %bitcast.170), channel_id=1, source_target_pairs={{0,64},{64,128},{128,192},{192,0},{1,65},{65,129},{129,193},{193,1... | collective-permute-start | bytes 1572872 | tf_op jit(solution)/shard_map/ppermute | solution.py:20
  142.1 2.8 %copy-start.1 = (bf16[512,512]{1,0:T(8,128)(2,1)S(1)}, bf16[512,512]{1,0:T(8,128)(2,1)}, u32[]{:S(2)}) copy-start(bf16[512,512]{1,0:T(8,128)(2,1)} %param.6) | copy-start | bytes 1572868
Sparse Core Ops, SparseCore 0:
  11.7 83.3 all-gather.1
where the time goes:
time: 152 us
  waiting for transfers between devices  64.6 us (42%)
  matrix products  23.6 us (16%)
  local copies, waits for them, and re-layouts  16.7 us (11%)
  starting transfers between devices  16.7 us (11%)
  other arithmetic  16.4 us (11%)
  between operations  13.7 us (9%)
    all_gather x1, waiting for transfers between devices, local(): arrived = lax.all_gather(outgoing, SEQ, axis=1, tiled=True)  40 us
    ppermute x7, waiting for transfers between devices, ring(): lax.ppermute(block, axis, [(i, (i + distance) % size) for i in range(size)])  24.6 us
    ppermute x2, starting transfers between devices, shift(): return lax.ppermute(block, axis, route)  8.48 us
    ppermute x7, starting transfers between devices, ring(): lax.ppermute(block, axis, [(i, (i + distance) % size) for i in range(size)])  8.26 us
    dot_general x3, matrix products, local(): jnp.dot(theirs, sibling_w[distance - 1], preferred_element_type=jnp.float32)  5.82 us
    reduce_sum x1, other arithmetic, local(): total_diag = jnp.sum(expo_diag, axis=2, keepdims=True)  5.65 us
    dot_general x3, matrix products, local(): jnp.dot(mine, fetched[distance - 1], preferred_element_type=jnp.float32)  4.51 us
    reduce_sum x1, other arithmetic, local(): jnp.sum(expo_vert, axis=2, keepdims=True)  3.83 us
  transfers between devices with their start and end apart: 10, of which 5 were waited for; matrix products, arithmetic and copies ran while one was open for 31% of the time, Pallas kernels for 0%

commit v1 on v0

--- a/solution.py
+++ b/solution.py
@@ -54,7 +54,8 @@
         selector = owned_here[None, :] & (slot_index[None, :] == jnp.arange(capacity)[:, None])
         picked = jnp.sum(jnp.where(selector, within_dev[None, :], 0), axis=1)
         outgoing = paired[:, picked].reshape(2, capacity * BLOCK_TOKENS, head_dim)
-        arrived = lax.all_gather(outgoing, SEQ, axis=1, tiled=True)
+        tall = lax.all_to_all(jnp.stack(lax.axis_size(SEQ) * [outgoing]), SEQ, 0, 0)
+        arrived = jnp.concatenate(tall, 1)
         rows_total, width = out_weight.shape
         col_width = width // heads_n
         half_rows = rows_total // core_n

time: 152 us -> 190 us (1.25)
  the two profiles are of different devices: /device:TPU:1 before, /device:TPU:37 now
where the time goes in v1:
time: 190 us; the launch traced here: 189 us
  waiting for transfers between devices  101 us (53%)
  local copies, waits for them, and re-layouts  24.1 us (13%)
  starting transfers between devices  23.6 us (12%)
  matrix products  23.6 us (12%)
  other arithmetic  16.3 us (9%)
    ppermute x2, waiting for transfers between devices, shift(): return lax.ppermute(block, axis, route)  81.3 us
    ppermute x7, waiting for transfers between devices, ring(): lax.ppermute(block, axis, [(i, (i + distance) % size) for i in range(size)])  19.5 us
    all_to_all x1, starting transfers between devices, local(): tall = lax.all_to_all(jnp.stack(lax.axis_size(SEQ) * [outgoing]), SEQ, 0, 0)  12.2 us
    ppermute x2, starting transfers between devices, shift(): return lax.ppermute(block, axis, route)  6.47 us
    dot_general x3, matrix products, local(): jnp.dot(theirs, sibling_w[distance - 1], preferred_element_type=jnp.float32)  5.82 us
    reduce_sum x1, other arithmetic, local(): total_diag = jnp.sum(expo_diag, axis=2, keepdims=True)  5.64 us
    ppermute x7, starting transfers between devices, ring(): lax.ppermute(block, axis, [(i, (i + distance) % size) for i in range(size)])  4.9 us
    all_to_all x1, local copies, waits for them, and re-layouts, local(): tall = lax.all_to_all(jnp.stack(lax.axis_size(SEQ) * [outgoing]), SEQ, 0, 0)  4.83 us
  transfers between devices with their start and end apart: 10, of which 3 were waited for; matrix products, arithmetic and copies ran while one was open for 27% of the time, Pallas kernels for 0%

profile of v1, /device:TPU:37, one launch (start us, length us, event | category | flops | bytes accessed | tf_op | source)
XLA Modules:
  0.0 188.8 jit_solution(4227775659782177344)
XLA Ops:
  1.2 1.7 pad_maximum_fusion.1
  2.9 1.5 gather_fusion
  4.4 3.1 %stack.27 = bf16[64,2,128,128]{3,2,1,0:T(8,128)(2,1)} broadcast(bf16[2,128,128]{2,1,0:T(8,128)(2,1)S(1)} %bitcast.182), dimensions={1,2,3} | broadcast | bytes 4259840 | tf_op jit(solution)/shard_map/stack | solution.py:57
  7.5 12.2 %all-to-all-start = ((bf16[64,2,128,128]{3,2,1,0:T(8,128)(2,1)}), bf16[64,2,128,128]{3,2,1,0:T(8,128)(2,1)}, u32[]{:S(2)}, u32[]{:S(2)}) async-start(bf16[64,2,128,128]{3,2,1,0:T(8,128)(2,1)} %stack.27), calls=%async_computation | async-start | bytes 8388608 | tf_op jit(solution)/shard_map/all_to_all | solution.py:57
  19.8 3.4 %collective-permute-start.1 = (bf16[2,8,64,128]{3,2,1,0:T(8,128)(2,1)}, bf16[2,8,64,128]{3,2,1,0:T(8,128)(2,1)}, u32[]{:S(2)}, u32[]{:S(2)}) collective-permute-start(bf16[2,8,64,128]{3,2,1,0:T(8,128)(2,1)} %pad_maximum_fusion.1), channel_id=1, source_target_pairs={{0,1},{1,2},{2,3},{3,4},{4,5},{5,6},{6,7},{7,8},{8,9},{9,10},{10,1... | collective-permute-start | bytes 786440 | tf_op jit(solution)/shard_map/ppermute | solution.py:16
  23.2 3.1 %collective-permute-start = (bf16[2,8,64,128]{3,2,1,0:T(8,128)(2,1)}, bf16[2,8,64,128]{3,2,1,0:T(8,128)(2,1)}, u32[]{:S(2)}, u32[]{:S(2)}) collective-permute-start(bf16[2,8,64,128]{3,2,1,0:T(8,128)(2,1)} %pad_maximum_fusion.1), channel_id=1, source_target_pairs={{0,2},{1,3},{2,4},{3,5},{4,6},{5,7},{6,8},{7,9},{8,10},{9,11},{10,... | collective-permute-start | bytes 786440 | tf_op jit(solution)/shard_map/ppermute | solution.py:16
  26.3 2.6 %fusion.57 = (bf16[256,1024]{1,0:T(8,128)(2,1)}, bf16[256,1024]{1,0:T(8,128)(2,1)}, bf16[256,1024]{1,0:T(8,128)(2,1)}) fusion(bf16[512,4096]{1,0:T(8,128)(2,1)} %param.11, s32[]{:T(128)S(6)} %select_n.128, s32[]{:T(128)S(6)} %select_n.130, s32[]{:T(128)S(6)} %select_n.135, s32[]{:T(128)S(6)} %select_n.133), kind=kLoop, calls=%fused_computation.100 | loop fusion | bytes 3145744 | tf_op jit(solution)/shard_map/dynamic_slice | solution.py:65
  29.1 2.5 %collective-permute-start.4 = (bf16[256,1024]{1,0:T(8,128)(2,1)}, bf16[256,1024]{1,0:T(8,128)(2,1)}, u32[]{:S(2)}, u32[]{:S(2)}) collective-permute-start(bf16[256,1024]{1,0:T(8,128)(2,1)} %get-tuple-element.13), channel_id=1, source_target_pairs={{0,128},{64,192},{128,0},{192,64},{1,129},{65,193},{129,1},{193,65... | collective-permute-start | bytes 1572872 | tf_op jit(solution)/shard_map/ppermute | solution.py:20
  32.9 2.1 %and.141 = pred[512,1536]{0,1:T(8,128)(4,1)S(1)} reshape(pred[8,64,24,64]{1,0,3,2:T(8,128)(4,1)S(1)} %tile.4) | data formatting | bytes 1572864 | tf_op jit(solution)/shard_map/and | solution.py:100
  39.9 81.3 %collective-permute-done = bf16[2,8,64,128]{3,2,1,0:T(8,128)(2,1)} collective-permute-done((bf16[2,8,64,128]{3,2,1,0:T(8,128)(2,1)}, bf16[2,8,64,128]{3,2,1,0:T(8,128)(2,1)}, u32[]{:S(2)}, u32[]{:S(2)}) %collective-permute-start) | collective-permute-done | bytes 262176 | tf_op jit(solution)/shard_map/ppermute | solution.py:16
  122.4 3.4 %fusion = (f32[4,512]{1,0:T(4,128)S(1)}, f32[1536,4,512]{2,0,1:T(8,128)S(1)}) fusion(pred[512,1536]{0,1:T(8,128)(4,1)S(1)} %and.141, pred[4,512,24]{1,2,0:T(8,128)(4,1)S(1)} %reshape.356, pred[4,512,24]{1,2,0:T(8,128)(4,1)S(1)} %reshape.354, bf16[1536,128,1]{1,0,2:T(8,128)(2,1)S(1)} %bitcast.170, bf16[512,512]{1,0:T(8,128)(2,1)S(1)} %copy-done), kind=kOutput, calls=%fused_computation.4 | convolution fusion | flops 821032960 | bytes 14393344 | tf_op jit(solution)/shard_map/htd,ud->htu/dot_general | solution.py:91
  125.8 5.6 %fusion.7 = (f32[4,512]{1,0:T(4,128)S(1)}, bf16[4,512,1536]{1,2,0:T(8,128)(2,1)}) fusion(f32[1536,4,512]{2,0,1:T(8,128)S(1)} %get-tuple-element.23, f32[4,512]{1,0:T(4,128)S(1)} %get-tuple-element.22, pred[512,1536]{0,1:T(8,128)(4,1)S(1)} %and.141, pred[4,512,24]{1,2,0:T(8,128)(4,1)S(1)} %reshape.356, pred[4,512,24]{1,2,0:T(8,128)(4,1)S(1)} %reshape.354), kind=kLoop, calls=%fused_computation.15 | loop fusion | flops 22018048 | bytes 19775488 | tf_op jit(solution)/shard_map/reduce_sum | solution.py:105
  131.4 2.7 %pad_maximum_fusion = bf16[3,256,1024]{2,1,0:T(8,128)(2,1)} fusion(bf16[1,256,1024]{2,1,0:T(8,128)(2,1)} %bitcast.31, bf16[1,256,1024]{2,1,0:T(8,128)(2,1)} %bitcast.30, bf16[1,256,1024]{2,1,0:T(8,128)(2,1)} %bitcast.29), kind=kLoop, calls=%fused_computation.21 | loop fusion | flops 1572864 | bytes 3145728 | tf_op jit(solution)/shard_map/stack | solution.py:69
  134.1 4.8 %copy.37 = bf16[64,2,128,128]{3,2,0,1:T(8,128)(2,1)} copy(bf16[64,2,128,128]{3,2,1,0:T(8,128)(2,1)} %all-to-all-done) | data formatting | bytes 8388608 | tf_op jit(solution)/shard_map/all_to_all | solution.py:57
  138.9 3.3 %gather_fusion.1 = bf16[64,2,64,128]{3,2,1,0:T(8,128)(2,1)S(1)} fusion(bf16[2,128,64,128]{3,2,1,0:T(8,128)(2,1)} %bitcast.166, s32[1024]{0:T(1024)} %pad_clamp_fusion), kind=kCustom, calls=%fused_computation.1 | custom fusion | bytes 4194560 | tf_op jit(solution)/shard_map/gather | solution.py:113
  142.9 3.0 %fusion.4 = (f32[4,512]{1,0:T(4,128)S(1)}, f32[4,1024,512]{2,1,0:T(8,128)S(1)}) fusion(pred[512,1024]{0,1:T(8,128)(4,1)S(1)} %and.144, s32[512]{0:T(512)S(1)} %copy-done.5, s32[4,1024]{1,0:T(4,128)S(1)} %copy-done.4, bf16[4,1024,128]{2,1,0:T(8,128)(2,1)S(1)} %bitcast.176, bf16[512,512]{1,0:T(8,128)(2,1)S(1)} %copy-done), kind=kOutput, calls=%fused_computation.11 | convolution fusion | flops 551548928 | bytes 10512384 | tf_op jit(solution)/shard_map/htd,hud->htu/dot_general | solution.py:117
  146.0 3.8 %fusion.9 = f32[4,512]{1,0:T(4,128)S(1)} fusion(f32[4,1024,512]{2,1,0:T(8,128)S(1)} %get-tuple-element.25, f32[4,512]{1,0:T(4,128)S(1)} %max.19, pred[512,1024]{0,1:T(8,128)(4,1)S(1)} %and.144, s32[512]{0:T(512)S(1)} %copy-done.5, s32[4,1024]{1,0:T(4,128)S(1)} %copy-done.4), kind=kLoop, calls=%fused_computation.17 | loop fusion | flops 16775168 | bytes 8947712 | tf_op jit(solution)/shard_map/reduce_sum | solution.py:130
  150.9 3.8 %divide_convert_fusion = bf16[512,4,128]{0,2,1:T(8,128)(2,1)S(1)} fusion(f32[512,4,128]{0,2,1:T(8,128)S(1)} %fusion.16, bf16[4,1024,128]{2,1,0:T(8,128)(2,1)S(1)} %bitcast.175, f32[4,1024,512]{2,1,0:T(8,128)S(1)} %get-tuple-element.25, f32[4,512]{1,0:T(4,128)S(1)} %max.19, f32[512,4]{0,1:T(4,128)S(1)} %get-tuple-element.5, s32[512]{0:T(512)S(1)} %copy-done.5, ...), kind=kOutput, calls=%fused_computation.28 | convolution fusion | flops 554434560 | bytes 11569152 | tf_op jit(solution)/shard_map/htu,hud->htd/dot_general | solution.py:131
  155.1 1.9 collective-permute-start.8
  157.0 1.9 %fusion.20 = f32[512,1024]{1,0:T(8,128)S(1)} fusion(bf16[512,512]{0,1:T(8,128)(2,1)S(1)} %bitcast.174, bf16[512,4096]{1,0:T(8,128)(2,1)} %param.11, s32[]{:T(128)S(6)} %select_n.127), kind=kOutput, calls=%fused_computation.26 | convolution fusion | flops 536870912 | bytes 3670020 | tf_op jit(solution)/shard_map/dot_general | solution.py:139
  158.9 10.5 %collective-permute-done.7 = bf16[512,512]{0,1:T(8,128)(2,1)S(1)} collective-permute-done((bf16[512,512]{0,1:T(8,128)(2,1)S(1)}, bf16[512,512]{0,1:T(8,128)(2,1)S(1)}, u32[]{:S(2)}, u32[]{:S(2)}) %collective-permute-start.7) | collective-permute-done | bytes 524320 | tf_op jit(solution)/shard_map/ppermute | solution.py:20
  170.9 1.5 fusion.27
  172.4 9.0 %collective-permute-done.2 = bf16[512,512]{0,1:T(8,128)(2,1)S(1)} collective-permute-done((bf16[512,512]{0,1:T(8,128)(2,1)S(1)}, bf16[512,512]{0,1:T(8,128)(2,1)S(1)}, u32[]{:S(2)}, u32[]{:S(2)}) %collective-permute-start.2) | collective-permute-done | bytes 524320 | tf_op jit(solution)/shard_map/ppermute | solution.py:20
  186.0 2.8 %add_convert_fusion = bf16[512,1024]{1,0:T(8,128)(2,1)} fusion(f32[512,1024]{1,0:T(8,128)S(1)} %fusion.32, f32[512,1024]{1,0:T(8,128)S(1)} %fusion.27, f32[512,1024]{1,0:T(8,128)S(1)} %fusion.35, f32[512,1024]{1,0:T(8,128)S(1)} %fusion.28, f32[512,1024]{1,0:T(8,128)S(1)} %fusion.20, f32[512,1024]{1,0:T(8,128)S(1)} %fusion.38, ...), kind=kOutput, calls=%fused_computation.20 | convolution fusion | flops 272105472 | bytes 14417924 | tf_op jit(solution)/shard_map/dot_general | solution.py:145
  (78 shorter events, 16.9 us)
Async XLA Ops:
  0.0 122.4 %copy-start = (bf16[512,512]{1,0:T(8,128)(2,1)S(1)}, bf16[512,512]{1,0:T(8,128)(2,1)}, u32[]{:S(2)}) copy-start(bf16[512,512]{1,0:T(8,128)(2,1)} %param.6) | copy-start | bytes 1572868
  7.5 126.6 %all-to-all-start = ((bf16[64,2,128,128]{3,2,1,0:T(8,128)(2,1)}), bf16[64,2,128,128]{3,2,1,0:T(8,128)(2,1)}, u32[]{:S(2)}, u32[]{:S(2)}) async-start(bf16[64,2,128,128]{3,2,1,0:T(8,128)(2,1)} %stack.27), calls=%async_computation | async-start | bytes 8388608 | tf_op jit(solution)/shard_map/all_to_all | solution.py:57
  19.8 11.9 %copy-start.6 = (s32[16,8]{0,1:T(8,128)S(1)}, s32[16,8]{0,1:T(8,128)}, u32[]{:S(2)}) copy-start(s32[16,8]{0,1:T(8,128)} %param.10) | copy-start | bytes 1540
  19.8 20.1 %collective-permute-start.1 = (bf16[2,8,64,128]{3,2,1,0:T(8,128)(2,1)}, bf16[2,8,64,128]{3,2,1,0:T(8,128)(2,1)}, u32[]{:S(2)}, u32[]{:S(2)}) collective-permute-start(bf16[2,8,64,128]{3,2,1,0:T(8,128)(2,1)} %pad_maximum_fusion.1), channel_id=1, source_target_pairs={{0,1},{1,2},{2,3},{3,4},{4,5},{5,6},{6,7},{7,8},{8,9},{9,10},{10,1... | collective-permute-start | bytes 786440 | tf_op jit(solution)/shard_map/ppermute | solution.py:16
  23.2 98.0 %collective-permute-start = (bf16[2,8,64,128]{3,2,1,0:T(8,128)(2,1)}, bf16[2,8,64,128]{3,2,1,0:T(8,128)(2,1)}, u32[]{:S(2)}, u32[]{:S(2)}) collective-permute-start(bf16[2,8,64,128]{3,2,1,0:T(8,128)(2,1)} %pad_maximum_fusion.1), channel_id=1, source_target_pairs={{0,2},{1,3},{2,4},{3,5},{4,6},{5,7},{6,8},{7,9},{8,10},{9,11},{10,... | collective-permute-start | bytes 786440 | tf_op jit(solution)/shard_map/ppermute | solution.py:16
  28.9 102.5 %collective-permute-start.5 = (bf16[256,1024]{1,0:T(8,128)(2,1)}, bf16[256,1024]{1,0:T(8,128)(2,1)}, u32[]{:S(2)}, u32[]{:S(2)}) collective-permute-start(bf16[256,1024]{1,0:T(8,128)(2,1)} %get-tuple-element.12), channel_id=1, source_target_pairs={{0,192},{64,0},{128,64},{192,128},{1,193},{65,1},{129,65},{193,129... | collective-permute-start | bytes 1572872 | tf_op jit(solution)/shard_map/ppermute | solution.py:20
  29.1 102.3 %collective-permute-start.4 = (bf16[256,1024]{1,0:T(8,128)(2,1)}, bf16[256,1024]{1,0:T(8,128)(2,1)}, u32[]{:S(2)}, u32[]{:S(2)}) collective-permute-start(bf16[256,1024]{1,0:T(8,128)(2,1)} %get-tuple-element.13), channel_id=1, source_target_pairs={{0,128},{64,192},{128,0},{192,64},{1,129},{65,193},{129,1},{193,65... | collective-permute-start | bytes 1572872 | tf_op jit(solution)/shard_map/ppermute | solution.py:20
  31.6 99.9 %collective-permute-start.3 = (bf16[256,1024]{1,0:T(8,128)(2,1)}, bf16[256,1024]{1,0:T(8,128)(2,1)}, u32[]{:S(2)}, u32[]{:S(2)}) collective-permute-start(bf16[256,1024]{1,0:T(8,128)(2,1)} %get-tuple-element.11), channel_id=1, source_target_pairs={{0,64},{64,128},{128,192},{192,0},{1,65},{65,129},{129,193},{193,1... | collective-permute-start | bytes 1572872 | tf_op jit(solution)/shard_map/ppermute | solution.py:20
  32.9 88.2 %copy-start.2 = (bf16[512,128]{1,0:T(8,128)(2,1)S(1)}, bf16[512,128]{1,0:T(8,128)(2,1)}, u32[]{:S(2)}) copy-start(bf16[512,128]{1,0:T(8,128)(2,1)} %param.8) | copy-start | bytes 393220
  35.1 86.1 %copy-start.3 = (bf16[512,128]{1,0:T(8,128)(2,1)S(1)}, bf16[512,128]{1,0:T(8,128)(2,1)}, u32[]{:S(2)}) copy-start(bf16[512,128]{1,0:T(8,128)(2,1)} %param.7) | copy-start | bytes 393220
  134.1 36.8 %collective-permute-start.6 = (bf16[3,256,1024]{2,1,0:T(8,128)(2,1)}, bf16[3,256,1024]{2,1,0:T(8,128)(2,1)}, u32[]{:S(2)}, u32[]{:S(2)}) collective-permute-start(bf16[3,256,1024]{2,1,0:T(8,128)(2,1)} %pad_maximum_fusion), channel_id=1, source_target_pairs={{0,1},{1,0},{2,3},{3,2},{4,5},{5,4},{6,7},{7,6},{8,9},{9,8},{10,11... | collective-permute-start | bytes 4718600 | tf_op jit(solution)/shard_map/ppermute | solution.py:20
  142.2 0.7 copy-start.4
  142.2 0.7 copy-start.5
  142.2 7.6 %slice-start = ((s8[6291456]{0:T(1024)(128)(4,1)}), s8[4194304]{0:T(1024)(128)(4,1)S(1)}, s32[]{:S(2)}) async-start(s8[6291456]{0:T(1024)(128)(4,1)} %bitcast.168), calls=%async_computation.1 | async-start | bytes 8388608
  142.9 6.9 %slice-start.1 = ((s8[6291456]{0:T(1024)(128)(4,1)}), s8[2097152]{0:T(1024)(128)(4,1)S(1)}, s32[]{:S(2)}) async-start(s8[6291456]{0:T(1024)(128)(4,1)} %bitcast.168), calls=%async_computation.2 | async-start | bytes 4194304
  154.8 14.6 %collective-permute-start.7 = (bf16[512,512]{0,1:T(8,128)(2,1)S(1)}, bf16[512,512]{0,1:T(8,128)(2,1)S(1)}, u32[]{:S(2)}, u32[]{:S(2)}) collective-permute-start(bf16[512,512]{0,1:T(8,128)(2,1)S(1)} %bitcast.171), channel_id=1, source_target_pairs={{0,128},{64,192},{128,0},{192,64},{1,129},{65,193},{129,1},{193,65... | collective-permute-start | bytes 1572872 | tf_op jit(solution)/shard_map/ppermute | solution.py:20
  155.1 29.4 %collective-permute-start.8 = (bf16[512,512]{0,1:T(8,128)(2,1)S(1)}, bf16[512,512]{0,1:T(8,128)(2,1)S(1)}, u32[]{:S(2)}, u32[]{:S(2)}) collective-permute-start(bf16[512,512]{0,1:T(8,128)(2,1)S(1)} %bitcast.172), channel_id=1, source_target_pairs={{0,192},{64,0},{128,64},{192,128},{1,193},{65,1},{129,65},{193,129... | collective-permute-start | bytes 1572872 | tf_op jit(solution)/shard_map/ppermute | solution.py:20
  157.0 24.5 %collective-permute-start.2 = (bf16[512,512]{0,1:T(8,128)(2,1)S(1)}, bf16[512,512]{0,1:T(8,128)(2,1)S(1)}, u32[]{:S(2)}, u32[]{:S(2)}) collective-permute-start(bf16[512,512]{0,1:T(8,128)(2,1)S(1)} %bitcast.173), channel_id=1, source_target_pairs={{0,64},{64,128},{128,192},{192,0},{1,65},{65,129},{129,193},{193,1... | collective-permute-start | bytes 1572872 | tf_op jit(solution)/shard_map/ppermute | solution.py:20
  186.0 2.8 %copy-start.1 = (bf16[512,512]{1,0:T(8,128)(2,1)S(1)}, bf16[512,512]{1,0:T(8,128)(2,1)}, u32[]{:S(2)}) copy-start(bf16[512,512]{1,0:T(8,128)(2,1)} %param.6) | copy-start | bytes 1572868
